TPU v7x, 512 devices: a whole 4x8x8 slice. The times are simulated.
512 devices in a mesh: tok: 64 (over x, z, core), mlp: 8 (over y).
Axes of the slice: x: 4, y: 8, z: 8, core: 2. Of those that a mesh axis runs over, the one named last changes fastest.
Arguments:
- queries: bfloat16 [4096, 7168], P('tok', 'mlp')
- fresh_token_keys: bfloat16 [4096, 1024], P('tok', 'mlp'), may hold values from -6 to 6
- fresh_token_values: bfloat16 [4096, 1024], P('tok', 'mlp'), may hold values from -6 to 6
- leaf_key_block: bfloat16 [20480, 1024], P('tok', 'mlp'), may hold values from -6 to 6
- leaf_value_block: bfloat16 [20480, 1024], P('tok', 'mlp'), may hold values from -6 to 6
- shared_key_block: bfloat16 [16384, 1024], P('tok', 'mlp'), may hold values from -6 to 6
- shared_value_block: bfloat16 [16384, 1024], P('tok', 'mlp'), may hold values from -6 to 6
- out_weight: bfloat16 [7168, 7168], P('mlp', 'tok'), may hold values from -0.0625 to 0.0625
- residual: bfloat16 [4096, 7168], P('mlp', 'tok'), may hold values from -2.5 to 2.5
- token_request: int32 [4096], replicated, may hold values from 0 to 63, as said below
- positions: int32 [4096], P('tok'), may hold values from 129 to 831, as said below
- parents: int32 [74], replicated, may hold values from -1 to 9, as said below
- node_lengths: int32 [74], replicated, may hold values from 1 to 256, as said below
- node_owner: int32 [74], replicated, may hold values from 0 to 63, as said below
Outputs:
- hidden: bfloat16 [4096, 7168], P('mlp', 'tok')
- leaf_key_output: bfloat16 [20480, 1024], P('tok', 'mlp')
- leaf_value_output: bfloat16 [20480, 1024], P('tok', 'mlp')
Inputs may be any that keep to these rules, and one draw needn't show every extreme that they name: `token_request`: index d of tok holds the 64 new tokens of the request whose leaf it owns (node_owner of that leaf is d), in some order. positions = node_lengths of the token's root, middle and leaf plus the token's rank among its request's new tokens; the ranks of one request are 0 to 63, each once. `parents`: nodes 0 to 1 are roots (parent -1), the next 8 are middle nodes with a root as parent, the last 64 are the leaves of requests 0, 1, ... with a middle node as parent; every root and middle node has a child; the leaf of request 0 lies below root 0. `node_lengths`: roots and middle nodes hold 64 to 256 tokens, root 0 and the middle node above leaf 0 exactly 256; leaves hold 1 to 256, leaf 0 exactly 256. `node_owner`: the 10 roots and middle nodes have different owners; the leaves' owners are a permutation of the indices of tok; a node's cache starts at row 0 of its owner's block.
All inputs are finite; a program needn't handle non-finite values.
Results may differ from a plain program's by a relative error of at most 0.012.
Values may be sent and summed in bfloat16 or wider, within the bound.
No kernel may reach another device: no remote copies, remote signals or barrier semaphores. Data moves between devices by JAX's collectives and lax.ppermute only.
A program may use at most 64 MiB of HBM per device.

v0:
```python
import math
import jax
import jax.numpy as jnp
from jax import lax
from jax.sharding import PartitionSpec as P

HEAD_SIZE = 128
ROOTS = 2
MIDS = 8
THETA = 5000000.0
NEG = -1e30


def apply_rotary(values, position, heads):
    width = values.shape[1] // heads
    half = width // 2
    table = values.astype(jnp.float32).reshape(values.shape[0], heads, width)
    freq = THETA ** (-(jnp.arange(half, dtype=jnp.float32) * 2.0) / width)
    angle = position.astype(jnp.float32)[:, None] * freq[None, :]
    cosine = jnp.cos(angle)[:, None, :]
    sine = jnp.sin(angle)[:, None, :]
    first = table[:, :, :half]
    second = table[:, :, half:]
    turned = jnp.concatenate(
        [first * cosine - second * sine, second * cosine + first * sine], axis=2
    )
    return turned.reshape(values.shape).astype(jnp.bfloat16)


def attend_key_block(queries4, keys, values, valid):
    scale = 1.0 / math.sqrt(queries4.shape[-1])
    scores = (
        jnp.einsum("sgqd,rgd->sgqr", queries4, keys, preferred_element_type=jnp.float32) * scale
    )
    allowed = valid[:, None, None, :]
    highest = jnp.max(jnp.where(allowed, scores, NEG), axis=3)
    weights = jnp.where(allowed, jnp.exp(scores - highest[..., None]), 0.0).astype(jnp.bfloat16)
    total = jnp.sum(weights.astype(jnp.float32), axis=3)
    output = jnp.einsum("sgqr,rgd->sgqd", weights, values, preferred_element_type=jnp.float32)
    return (highest, total, output)


def merge_state(state, block):
    high_a, total_a, out_a = state
    running_peak_b, running_sum_b, partial_output_b = block
    highest = jnp.maximum(high_a, running_peak_b)
    scale_a = jnp.exp(high_a - highest)
    scale_b = jnp.exp(running_peak_b - highest)
    return (
        highest,
        scale_a * total_a + scale_b * running_sum_b,
        scale_a[..., None] * out_a + scale_b[..., None] * partial_output_b,
    )


def lookup(table, index):
    return jnp.sum(jnp.where(jnp.arange(table.shape[0]) == index, table, 0))


def body(
    queries,
    fresh_token_keys,
    fresh_token_values,
    leaf_key_block,
    leaf_value_block,
    shared_key_block,
    shared_value_block,
    out_weight,
    residual,
    token_request,
    positions,
    parents,
    node_lengths,
    node_owner,
):
    my_index = lax.axis_index("tok")
    tok_rows = queries.shape[0]
    width = HEAD_SIZE
    q_heads = queries.shape[1] // width
    kv_heads = fresh_token_keys.shape[1] // width
    group = q_heads // kv_heads
    kv_width = kv_heads * width
    shared_count = ROOTS + MIDS
    query_turned = apply_rotary(queries, positions, q_heads)
    key_turned = apply_rotary(fresh_token_keys, positions, kv_heads)
    my_request = lax.dynamic_slice_in_dim(token_request, my_index * tok_rows, 1)[0]
    leaf_node = shared_count + my_request
    middle = lookup(parents, leaf_node)
    root = lookup(parents, middle)
    leaf_length = lookup(node_lengths, leaf_node)
    root_length = lookup(node_lengths, root)
    middle_length = lookup(node_lengths, middle)
    new_index = positions - root_length - middle_length - leaf_length
    leaf_rows = leaf_key_block.shape[0]
    row_ids = jnp.arange(leaf_rows)
    place = (row_ids[:, None] == (leaf_length + new_index)[None, :]).astype(jnp.bfloat16)
    pairs = jnp.concatenate([key_turned, fresh_token_values], axis=1)
    placed = jnp.dot(place, pairs, preferred_element_type=jnp.float32).astype(jnp.bfloat16)
    keep = row_ids[:, None] < leaf_length
    leaf_key_output = jnp.where(keep, leaf_key_block, placed[:, :kv_width])
    leaf_value_output = jnp.where(keep, leaf_value_block, placed[:, kv_width:])
    token_queries = query_turned.reshape(tok_rows, kv_heads, group, width)
    leaf_row_mask = row_ids[None, :] < (leaf_length + new_index + 1)[:, None]
    leaf_state = attend_key_block(
        token_queries,
        leaf_key_output.reshape(leaf_rows, kv_heads, width),
        leaf_value_output.reshape(leaf_rows, kv_heads, width),
        leaf_row_mask,
    )
    node_rows = shared_key_block.shape[0]
    root_owner = lookup(node_owner, root)
    middle_owner = lookup(node_owner, middle)
    gathered = (
        lax.all_gather(shared_key_block, "tok", axis=0, tiled=True),
        lax.all_gather(shared_value_block, "tok", axis=0, tiled=True),
    )
    root_keys = lax.dynamic_slice_in_dim(gathered[0], root_owner * node_rows, node_rows, 0)
    root_values = lax.dynamic_slice_in_dim(gathered[1], root_owner * node_rows, node_rows, 0)
    middle_keys = lax.dynamic_slice_in_dim(gathered[0], middle_owner * node_rows, node_rows, 0)
    middle_values = lax.dynamic_slice_in_dim(gathered[1], middle_owner * node_rows, node_rows, 0)
    node_ids = jnp.arange(node_rows)
    both_keys = jnp.concatenate([root_keys, middle_keys], axis=0).reshape(
        2 * node_rows, kv_heads, width
    )
    both_values = jnp.concatenate([root_values, middle_values], axis=0).reshape(
        2 * node_rows, kv_heads, width
    )
    both_valid = jnp.concatenate([node_ids < root_length, node_ids < middle_length], axis=0)
    shared_state = attend_key_block(token_queries, both_keys, both_values, both_valid[None, :])
    final = merge_state(shared_state, leaf_state)
    attended_local = (
        (final[2] / final[1][..., None]).reshape(tok_rows, q_heads * width).astype(jnp.bfloat16)
    )
    projected = jnp.dot(
        lax.all_gather(attended_local, "tok", axis=0, tiled=True),
        out_weight,
        preferred_element_type=jnp.float32,
    )
    summed = lax.psum_scatter(projected, "mlp", scatter_dimension=0, tiled=True)
    hidden = (residual.astype(jnp.float32) + summed).astype(jnp.bfloat16)
    return (hidden, leaf_key_output, leaf_value_output)


def solution(mesh):
    placed = (
        P("tok", "mlp"),
        P("tok", "mlp"),
        P("tok", "mlp"),
        P("tok", "mlp"),
        P("tok", "mlp"),
        P("tok", "mlp"),
        P("tok", "mlp"),
        P("mlp", "tok"),
        P("mlp", "tok"),
        P(),
        P("tok"),
        P(),
        P(),
        P(),
    )
    return jax.shard_map(
        body,
        mesh=mesh,
        in_specs=placed,
        out_specs=(P("mlp", "tok"), P("tok", "mlp"), P("tok", "mlp")),
        check_vma=False,
    )
```

profile of v0, /device:TPU:2, one launch (start us, length us, event | category | flops | bytes accessed | tf_op | source)
XLA Modules:
  0.0 330.6 jit_solution(14689822310884693069)
XLA Ops:
  7.2 0.0 copy-start
  7.2 0.0 all-gather.4.cloned.1.call-start
  7.2 0.7 all-gather.4.cloned.1.call-update
  7.9 0.0 all-gather.6.cloned.1.call-start
  8.0 0.7 all-gather.6.cloned.1.call-update
  8.7 0.0 all-gather.8.cloned.1.call-start
  8.7 1.3 dynamic_slice.15
  10.6 1.3 fusion.30
  11.9 1.9 select_reduce_fusion.4
  13.9 2.7 fusion.31
  17.7 1.0 reshape.252
  18.8 0.6 iota_compare_fusion.3
  19.4 0.6 iota_compare_fusion.5
  20.0 0.6 iota_compare_fusion.4
  20.6 1.9 broadcast_add_fusion
  22.5 0.7 bitcast_convert_fusion
  23.2 0.2 fusion.22
  23.4 0.1 maximum_bitcast_fusion.4
  23.5 0.1 iota_compare_fusion.2
  23.6 0.2 multiply_cosine_fusion.1
  23.8 0.9 convolution_convert_fusion
  24.7 1.1 slice_select_fusion
  25.8 0.0 copy-start.1
  25.8 0.0 copy-start.3
  25.8 0.1 fusion.42
  25.9 0.1 subtract_convert_fusion
  26.0 0.4 select_reduce_fusion.1
  26.4 0.3 convert_reduce_fusion.1
  26.7 73.5 %all-gather.4.cloned.1.call-done = bf16[16384,128]{1,0:T(8,128)(2,1)} async-done(((bf16[256,128]{1,0:T(8,128)(2,1)}), bf16[16384,128]{1,0:T(8,128)(2,1)}) %all-gather.4.cloned.1.call-update) | async-done | bytes 4194320 | tf_op jit(solution)/shard_map/all_gather | solution.py:114
  100.2 0.9 constant_dynamic-slice_fusion.3
  101.1 0.4 select_reduce_fusion
  101.5 0.3 convert_reduce_fusion
  101.8 83.5 %all-gather.6.cloned.1.call-done = bf16[16384,128]{1,0:T(8,128)(2,1)} async-done(((bf16[256,128]{1,0:T(8,128)(2,1)}), bf16[16384,128]{1,0:T(8,128)(2,1)}) %all-gather.6.cloned.1.call-update) | async-done | bytes 4194320 | tf_op jit(solution)/shard_map/all_gather | solution.py:115
  185.4 0.9 constant_dynamic-slice_fusion.1
  186.3 0.3 fusion.5
  186.6 0.3 fusion.7
  186.9 0.0 copy-done.1
  186.9 0.0 copy-done.3
  186.9 0.1 copy.19
  187.0 0.7 copy.28
  187.7 0.0 all-gather.8.cloned.1.call-update
  187.7 0.0 copy-start.2
  187.7 0.0 reduce-scatter.2.cloned.1.call-start
  187.8 86.2 %all-gather.8.cloned.1.call-done = bf16[4096,896]{1,0:T(8,128)(2,1)} async-done(((bf16[64,896]{1,0:T(8,128)(2,1)}), bf16[4096,896]{1,0:T(8,128)(2,1)}) %all-gather.8.cloned.1.call-update) | async-done | bytes 7340048 | tf_op jit(solution)/shard_map/all_gather | solution.py:135
  274.0 0.0 copy-done
  274.0 6.7 %fusion.43 = f32[4096,112]{0,1:T(8,128)} fusion(bf16[4096,896]{1,0:T(8,128)(2,1)} %all-gather.8.cloned.1.call-done, bf16[896,112]{0,1:T(8,128)(2,1)S(1)} %copy-done), kind=kOutput, calls=%fused_computation.91 | convolution fusion | flops 822083584 | bytes 9375744 | tf_op jit(solution)/shard_map/dot_general | solution.py:134
  280.7 0.0 reduce-scatter.2.cloned.1.call-update
  280.7 41.7 %reduce-scatter.2.cloned.1.call-done = f32[512,112]{0,1:T(8,128)} async-done(((f32[4096,112]{0,1:T(8,128)}), f32[512,112]{0,1:T(8,128)}) %reduce-scatter.2.cloned.1.call-update) | async-done | bytes 229392 | tf_op jit(solution)/shard_map/reduce_scatter | solution.py:139
  322.4 0.0 copy-done.2
  322.4 1.6 add_convert_fusion
  (3 shorter events, 0.0 us)
Async XLA Ops:
  7.2 266.8 %copy-start = (bf16[896,112]{0,1:T(8,128)(2,1)S(1)}, bf16[896,112]{0,1:T(8,128)(2,1)}, u32[]{:S(2)}) copy-start(bf16[896,112]{0,1:T(8,128)(2,1)} %param.21) | copy-start | bytes 602116
  7.2 93.0 %all-gather.4.cloned.1.call-start = ((), (), s32[]{:S(2)}) async-start(), calls=%async_computation.1 | async-start | bytes 4259840 | tf_op jit(solution)/shard_map/all_gather | solution.py:114
  7.9 177.5 %all-gather.6.cloned.1.call-start = ((), (), s32[]{:S(2)}) async-start(), calls=%async_computation.2 | async-start | bytes 4259840 | tf_op jit(solution)/shard_map/all_gather | solution.py:115
  8.7 265.3 %all-gather.8.cloned.1.call-start = ((), (), s32[]{:S(2)}) async-start(), calls=%async_computation.3 | async-start | bytes 7454720 | tf_op jit(solution)/shard_map/all_gather | solution.py:135
  25.8 161.2 %copy-start.1 = (bf16[320,128]{1,0:T(8,128)(2,1)}, bf16[320,128]{1,0:T(8,128)(2,1)S(1)}, u32[]{:S(2)}) copy-start(bf16[320,128]{1,0:T(8,128)(2,1)S(1)} %get-tuple-element.22) | copy-start | bytes 245764
  25.8 161.2 %copy-start.3 = (bf16[320,128]{1,0:T(8,128)(2,1)}, bf16[320,128]{1,0:T(8,128)(2,1)S(1)}, u32[]{:S(2)}) copy-start(bf16[320,128]{1,0:T(8,128)(2,1)S(1)} %get-tuple-element.21) | copy-start | bytes 245764
  187.7 134.7 %copy-start.2 = (bf16[512,112]{0,1:T(8,128)(2,1)S(1)}, bf16[512,112]{0,1:T(8,128)(2,1)}, u32[]{:S(2)}) copy-start(bf16[512,112]{0,1:T(8,128)(2,1)} %param.22) | copy-start | bytes 344068
  187.7 134.7 %reduce-scatter.2.cloned.1.call-start = ((), (), s32[]{:S(2)}) async-start(), calls=%async_computation.4 | async-start | bytes 2064384 | tf_op jit(solution)/shard_map/reduce_scatter | solution.py:139
Sparse Core Ops, SparseCore 0:
  11.4 88.7 all-gather.3
  103.5 81.7 all-gather.5
  189.3 84.6 all-gather.7
  280.9 41.5 reduce-scatter.1
where the time goes:
time: 331 us
  waiting for transfers between devices  286 us (86%)
  between operations  15.8 us (5%)
  other arithmetic  14.3 us (4%)
  matrix products  9.1 us (3%)
  local copies, waits for them, and re-layouts  4.98 us (2%)
    all_gather x1, waiting for transfers between devices, body(): lax.all_gather(attended_local, 'tok', axis=0, tiled=True)  86.2 us
    all_gather x1, waiting for transfers between devices, body(): lax.all_gather(shared_value_block, 'tok', axis=0, tiled=True)  83.5 us
    all_gather x1, waiting for transfers between devices, body(): lax.all_gather(shared_key_block, 'tok', axis=0, tiled=True)  73.5 us
    reduce_scatter x1, waiting for transfers between devices, body(): summed = lax.psum_scatter(projected, 'mlp', scatter_dimension=0, tiled=True)  41.7 us
    dot_general x1, matrix products, body(): jnp.dot(lax.all_gather(attended_local, 'tok', axis=0, tiled=True), out_we...  6.74 us
  transfers between devices with their start and end apart: 4, of which 4 were waited for; matrix products, arithmetic and copies ran while one was open for 5% of the time, Pallas kernels for 0%

commit v1 on v0

--- a/solution.py
+++ b/solution.py
@@ -9,6 +9,14 @@
 MIDS = 8
 THETA = 5000000.0
 NEG = -1e30
+
+
+def search_the_sites(v0, which_dim):
+    piece_next = lax.axis_size("tok")
+    h_now = jnp.stack(piece_next * [v0], axis=0)
+    x_new = lax.all_to_all(h_now, "tok", 0, 0)
+    mat_out = jnp.concatenate(x_new, axis=which_dim)
+    return mat_out
 
 
 def apply_rotary(values, position, heads):
@@ -111,7 +119,7 @@
     root_owner = lookup(node_owner, root)
     middle_owner = lookup(node_owner, middle)
     gathered = (
-        lax.all_gather(shared_key_block, "tok", axis=0, tiled=True),
+        search_the_sites(shared_key_block, 0),
         lax.all_gather(shared_value_block, "tok", axis=0, tiled=True),
     )
     root_keys = lax.dynamic_slice_in_dim(gathered[0], root_owner * node_rows, node_rows, 0)

time: 331 us -> 279 us (0.84)
  waiting for transfers between devices: 286 us -> 222 us
  starting transfers between devices: 0.16 us -> 14.3 us
  other arithmetic: 14.3 us -> 10.3 us
    all_to_all x0 -> x1, waiting for transfers between devices: none -> 93.4 us  [search_the_sites(): x_new = lax.all_to_all(h_now, 'tok', 0, 0)]
    all_gather x1, waiting for transfers between devices: 83.5 us -> 0.02 us  [body(): lax.all_gather(shared_value_block, 'tok', axis=0, tiled=True)]
    all_gather x1 -> x0, waiting for transfers between devices: 73.5 us -> none  [body(): lax.all_gather(shared_key_block, 'tok', axis=0, tiled=True)]
    all_to_all x0 -> x1, starting transfers between devices: none -> 14.2 us  [search_the_sites(): x_new = lax.all_to_all(h_now, 'tok', 0, 0)]
    another operation x0 -> x1, local copies, waits for them, and re-layouts: none -> 3.86 us  [search_the_sites(): h_now = jnp.stack(piece_next * [v0], axis=0)]
  transfers between devices with their start and end apart: 4 -> 4, of which waited for: 4 -> 3; matrix products, arithmetic and copies ran while one was open for 5% -> 4% of each run, Pallas kernels for 0% -> 0%
where the time goes in v1:
time: 279 us
  waiting for transfers between devices  222 us (80%)
  between operations  16 us (6%)
  starting transfers between devices  14.3 us (5%)
  other arithmetic  10.3 us (4%)
  matrix products  8.37 us (3%)
  local copies, waits for them, and re-layouts  8 us (3%)
    all_to_all x1, waiting for transfers between devices, search_the_sites(): x_new = lax.all_to_all(h_now, 'tok', 0, 0)  93.4 us
    all_gather x1, waiting for transfers between devices, body(): lax.all_gather(attended_local, 'tok', axis=0, tiled=True)  86 us
    reduce_scatter x1, waiting for transfers between devices, body(): summed = lax.psum_scatter(projected, 'mlp', scatter_dimension=0, tiled=True)  41.7 us
    all_to_all x1, starting transfers between devices, search_the_sites(): x_new = lax.all_to_all(h_now, 'tok', 0, 0)  14.2 us
    dot_general x1, matrix products, body(): jnp.dot(lax.all_gather(attended_local, 'tok', axis=0, tiled=True), out_we...  6.73 us
  transfers between devices with their start and end apart: 4, of which 3 were waited for; matrix products, arithmetic and copies ran while one was open for 4% of the time, Pallas kernels for 0%

profile of v1, /device:TPU:2, one launch (start us, length us, event | category | flops | bytes accessed | tf_op | source)
XLA Modules:
  0.0 278.8 jit_solution(16083135580632722029)
XLA Ops:
  7.2 0.0 copy-start
  7.2 3.9 %stack.2 = bf16[64,256,128]{2,1,0:T(8,128)(2,1)} broadcast(bf16[256,128]{1,0:T(8,128)(2,1)} %param.19), dimensions={1,2} | broadcast | bytes 4259840 | tf_op jit(solution)/shard_map/stack | solution.py:16
  11.0 0.0 copy-start.12
  11.1 0.0 copy-start.11
  11.1 0.0 copy-start.7
  11.1 0.0 copy-start.8
  11.1 0.0 copy-start.4
  11.1 0.0 copy-start.5
  11.1 14.2 %all-to-all-start = ((bf16[64,256,128]{2,1,0:T(8,128)(2,1)}), bf16[64,256,128]{2,1,0:T(8,128)(2,1)}, u32[]{:S(2)}, u32[]{:S(2)}) async-start(bf16[64,256,128]{2,1,0:T(8,128)(2,1)} %stack.2), calls=%async_computation | async-start | bytes 8388608 | tf_op jit(solution)/shard_map/all_to_all | solution.py:17
  25.3 0.0 all-gather.3.cloned.1.call-start
  25.4 0.7 all-gather.3.cloned.1.call-update
  26.1 0.0 all-gather.5.cloned.1.call-start
  26.1 1.3 dynamic_slice.15
  28.0 0.0 copy-done.12
  28.1 0.6 fusion.30
  28.7 1.3 select_reduce_fusion.4
  30.0 0.0 copy-done.9
  30.0 0.0 copy-done.10
  30.0 2.0 fusion.31
  33.3 0.0 copy-done.3
  33.3 0.1 reshape.258
  33.5 0.7 iota_compare_fusion.4
  34.2 0.6 iota_compare_fusion.5
  34.8 0.7 iota_compare_fusion.3
  35.5 0.0 copy-done.11
  35.5 1.3 broadcast_add_fusion
  36.8 0.0 copy-done.7
  36.8 0.2 fusion.22
  37.0 0.1 maximum_bitcast_fusion.4
  37.1 0.1 iota_compare_fusion.2
  37.2 0.2 multiply_cosine_fusion.1
  37.4 0.0 copy-done.8
  37.4 0.2 convolution_convert_fusion
  37.6 0.0 copy-done.4
  37.6 0.0 copy-done.5
  37.6 0.1 slice_select_fusion
  37.7 0.0 copy-start.1
  37.7 0.0 copy-start.6
  37.8 0.1 fusion.42
  37.9 0.1 subtract_convert_fusion
  38.0 0.4 select_reduce_fusion.1
  38.4 0.3 convert_reduce_fusion.1
  38.7 93.4 %all-to-all-done = bf16[64,256,128]{2,1,0:T(8,128)(2,1)} async-done(((bf16[64,256,128]{2,1,0:T(8,128)(2,1)}), bf16[64,256,128]{2,1,0:T(8,128)(2,1)}, u32[]{:S(2)}, u32[]{:S(2)}) %all-to-all-start) | async-done | bytes 4194336 | tf_op jit(solution)/shard_map/all_to_all | solution.py:17
  132.1 0.9 constant_dynamic-slice_fusion.3
  133.0 0.4 select_reduce_fusion
  133.4 0.3 convert_reduce_fusion
  133.7 0.0 all-gather.3.cloned.1.call-done
  133.8 0.9 constant_dynamic-slice_fusion.1
  134.7 0.3 fusion.5
  135.0 0.3 fusion.7
  135.3 0.0 copy-done.1
  135.3 0.0 copy-done.6
  135.3 0.1 copy.19
  135.4 0.7 copy.28
  136.1 0.0 all-gather.5.cloned.1.call-update
  136.1 0.0 copy-start.2
  136.1 0.0 reduce-scatter.2.cloned.1.call-start
  136.2 86.0 %all-gather.5.cloned.1.call-done = bf16[4096,896]{1,0:T(8,128)(2,1)} async-done(((bf16[64,896]{1,0:T(8,128)(2,1)}), bf16[4096,896]{1,0:T(8,128)(2,1)}) %all-gather.5.cloned.1.call-update) | async-done | bytes 7340048 | tf_op jit(solution)/shard_map/all_gather | solution.py:143
  222.2 0.0 copy-done
  222.2 6.7 %fusion.43 = f32[4096,112]{0,1:T(8,128)} fusion(bf16[4096,896]{1,0:T(8,128)(2,1)} %all-gather.5.cloned.1.call-done, bf16[896,112]{0,1:T(8,128)(2,1)S(1)} %copy-done), kind=kOutput, calls=%fused_computation.91 | convolution fusion | flops 822083584 | bytes 9375744 | tf_op jit(solution)/shard_map/dot_general | solution.py:142
  229.0 0.0 reduce-scatter.2.cloned.1.call-update
  229.0 41.7 %reduce-scatter.2.cloned.1.call-done = f32[512,112]{0,1:T(8,128)} async-done(((f32[4096,112]{0,1:T(8,128)}), f32[512,112]{0,1:T(8,128)}) %reduce-scatter.2.cloned.1.call-update) | async-done | bytes 229392 | tf_op jit(solution)/shard_map/reduce_scatter | solution.py:147
  270.6 0.0 copy-done.2
  270.7 1.6 add_convert_fusion
  (7 shorter events, 0.0 us)
Async XLA Ops:
  7.2 215.1 %copy-start = (bf16[896,112]{0,1:T(8,128)(2,1)S(1)}, bf16[896,112]{0,1:T(8,128)(2,1)}, u32[]{:S(2)}) copy-start(bf16[896,112]{0,1:T(8,128)(2,1)} %param.21) | copy-start | bytes 602116
  11.0 17.0 %copy-start.12 = (s32[74]{0:T(128)S(1)}, s32[74]{0:T(128)}, u32[]{:S(2)}) copy-start(s32[74]{0:T(128)} %param.25) | copy-start | bytes 892
  11.0 18.9 %copy-start.9 = (s32[74]{0:T(128)S(1)}, s32[74]{0:T(128)}, u32[]{:S(2)}) copy-start(s32[74]{0:T(128)} %param.26) | copy-start | bytes 892
  11.0 18.9 %copy-start.10 = (s32[74]{0:T(128)S(1)}, s32[74]{0:T(128)}, u32[]{:S(2)}) copy-start(s32[74]{0:T(128)} %param.27) | copy-start | bytes 892
  11.1 22.2 %copy-start.3 = (bf16[64,896]{1,0:T(8,128)(2,1)S(1)}, bf16[64,896]{1,0:T(8,128)(2,1)}, u32[]{:S(2)}) copy-start(bf16[64,896]{1,0:T(8,128)(2,1)} %param.14) | copy-start | bytes 344068
  11.1 24.4 %copy-start.11 = (s32[64]{0:T(128)S(1)}, s32[64]{0:T(128)}, u32[]{:S(2)}) copy-start(s32[64]{0:T(128)} %param.24) | copy-start | bytes 772
  11.1 25.8 %copy-start.7 = (bf16[64,128]{1,0:T(8,128)(2,1)S(1)}, bf16[64,128]{1,0:T(8,128)(2,1)}, u32[]{:S(2)}) copy-start(bf16[64,128]{1,0:T(8,128)(2,1)} %param.15) | copy-start | bytes 49156
  11.1 26.3 %copy-start.8 = (bf16[64,128]{1,0:T(8,128)(2,1)S(1)}, bf16[64,128]{1,0:T(8,128)(2,1)}, u32[]{:S(2)}) copy-start(bf16[64,128]{1,0:T(8,128)(2,1)} %param.16) | copy-start | bytes 49156
  11.1 26.5 %copy-start.4 = (bf16[320,128]{1,0:T(8,128)(2,1)S(1)}, bf16[320,128]{1,0:T(8,128)(2,1)}, u32[]{:S(2)}) copy-start(bf16[320,128]{1,0:T(8,128)(2,1)} %param.18) | copy-start | bytes 245764
  11.1 26.5 %copy-start.5 = (bf16[320,128]{1,0:T(8,128)(2,1)S(1)}, bf16[320,128]{1,0:T(8,128)(2,1)}, u32[]{:S(2)}) copy-start(bf16[320,128]{1,0:T(8,128)(2,1)} %param.17) | copy-start | bytes 245764
  11.1 121.0 %all-to-all-start = ((bf16[64,256,128]{2,1,0:T(8,128)(2,1)}), bf16[64,256,128]{2,1,0:T(8,128)(2,1)}, u32[]{:S(2)}, u32[]{:S(2)}) async-start(bf16[64,256,128]{2,1,0:T(8,128)(2,1)} %stack.2), calls=%async_computation | async-start | bytes 8388608 | tf_op jit(solution)/shard_map/all_to_all | solution.py:17
  25.3 108.4 %all-gather.3.cloned.1.call-start = ((), (), s32[]{:S(2)}) async-start(), calls=%async_computation.2 | async-start | bytes 4259840 | tf_op jit(solution)/shard_map/all_gather | solution.py:123
  26.1 196.2 %all-gather.5.cloned.1.call-start = ((), (), s32[]{:S(2)}) async-start(), calls=%async_computation.3 | async-start | bytes 7454720 | tf_op jit(solution)/shard_map/all_gather | solution.py:143
  37.7 97.6 %copy-start.1 = (bf16[320,128]{1,0:T(8,128)(2,1)}, bf16[320,128]{1,0:T(8,128)(2,1)S(1)}, u32[]{:S(2)}) copy-start(bf16[320,128]{1,0:T(8,128)(2,1)S(1)} %get-tuple-element.22) | copy-start | bytes 245764
  37.7 97.6 %copy-start.6 = (bf16[320,128]{1,0:T(8,128)(2,1)}, bf16[320,128]{1,0:T(8,128)(2,1)S(1)}, u32[]{:S(2)}) copy-start(bf16[320,128]{1,0:T(8,128)(2,1)S(1)} %get-tuple-element.21) | copy-start | bytes 245764
  136.1 134.5 %copy-start.2 = (bf16[512,112]{0,1:T(8,128)(2,1)S(1)}, bf16[512,112]{0,1:T(8,128)(2,1)}, u32[]{:S(2)}) copy-start(bf16[512,112]{0,1:T(8,128)(2,1)} %param.22) | copy-start | bytes 344068
  136.1 134.5 %reduce-scatter.2.cloned.1.call-start = ((), (), s32[]{:S(2)}) async-start(), calls=%async_computation.4 | async-start | bytes 2064384 | tf_op jit(solution)/shard_map/reduce_scatter | solution.py:147
Sparse Core Ops, SparseCore 0:
  29.5 101.8 all-gather.2
  136.2 85.9 all-gather.4
  229.1 41.5 reduce-scatter.1
